TPU v7x, 32 devices: a whole 2x2x4 slice. The times are simulated.
32 devices in a mesh: day: 4 (over z), dom: 8 (over y, x, core).
Axes of the slice: x: 2, y: 2, z: 4, core: 2. Of those that a mesh axis runs over, the one named last changes fastest.
Arguments:
- node_states: bfloat16 [16, 2048, 256], P('day', 'dom'), may hold values from -12 to 12
- edge_source: int32 [16, 8192], P('day', 'dom'), may hold values from 0 to 383
- edge_target: int32 [16, 8192], P('day', 'dom'), may hold values from 0 to 255
- halo_rows: int32 [16, 1024], P('day', 'dom'), may hold values from 0 to 255
- halo_count: int32 [16, 8], P('day', 'dom'), may hold values from 1 to 128, 640 in all within a row
- w_message: bfloat16 [256, 256], replicated, may hold values from -0.375 to 0.375
- w_query: bfloat16 [256, 256], replicated, may hold values from -1 to 1, as said below
- w_key: bfloat16 [256, 256], replicated, may hold values from -1 to 1, as said below
- w_value: bfloat16 [256, 256], replicated, may hold values from -0.375 to 0.375
- cotangent: bfloat16 [16, 8, 4, 64, 256], P(None, 'dom', 'day'), may hold values from -6 to 6
Outputs:
- state_grad: float32 [16, 2048, 256], P('day', 'dom')
- grad_message: float32 [256, 256], replicated
- grad_query: float32 [256, 256], replicated
- grad_key: float32 [256, 256], replicated
- grad_value: float32 [256, 256], replicated
Inputs may be any that keep to these rules, and one draw needn't show every extreme that they name: `edge_source`: indices of the extended rows: below 256 a partition's own account, from 256 on a received halo slot. `halo_rows`: rows of the sending partition's own block; repeats allowed. `halo_count`: on every day some partition has all 128 slots live. `w_query`: entries of order 256 ** -0.5. `w_key`: entries of order 256 ** -0.5.
All inputs are finite; a program needn't handle non-finite values. No bound on the sum of `halo_count` on one device may be relied on, other than what follows from the above.
Results may differ from a plain program's by a relative error of at most 0.004.
The roundings to bfloat16 on the way count: a program that leaves them out, or rounds other values in their place, can miss the bound.
Values may be sent and summed in bfloat16 or wider, within the bound.
No kernel may reach another device: no remote copies, remote signals or barrier semaphores. Data moves between devices by JAX's collectives and lax.ppermute only.
A program may use at most 64 MiB of HBM per device.

v0:
```python
import jax
import jax.numpy as jnp
from jax import lax
from jax.sharding import PartitionSpec as P

HEADS = 4


def from_behind(value, axis, steps):
    count = lax.axis_size(axis)
    pairs = [(source, (source + steps) % count) for source in range(count)]
    return lax.ppermute(value, axis, pairs)


def _power_of_two(count):
    return count > 0 and count & count - 1 == 0


def tree_sum(values, axes):
    sizes = [lax.axis_size(axis) for axis in axes]
    flat = jnp.concatenate([value.reshape(-1) for value in values])
    total = 1
    for size in sizes:
        total *= size
    if not all((_power_of_two(size) for size in sizes)) or flat.shape[0] % total:
        return lax.psum(tuple(values), axes)
    steps = [
        (axis, bit)
        for axis, size in zip(axes, sizes)
        for bit in [1 << k for k in range(size.bit_length() - 1)]
    ]
    for axis, bit in steps:
        side = lax.axis_index(axis) // bit % 2
        halves = flat.reshape(2, -1)
        keep = jnp.where(side == 0, halves[0], halves[1])
        send = jnp.where(side == 0, halves[1], halves[0])
        pairs = [(source, source ^ bit) for source in range(lax.axis_size(axis))]
        flat = keep + lax.ppermute(send, axis, pairs)
    for axis, bit in reversed(steps):
        side = lax.axis_index(axis) // bit % 2
        pairs = [(source, source ^ bit) for source in range(lax.axis_size(axis))]
        other = lax.ppermute(flat, axis, pairs)
        flat = jnp.where(side == 0, jnp.concatenate([flat, other]), jnp.concatenate([other, flat]))
    results, start = ([], 0)
    for value in values:
        results.append(flat[start : start + value.size].reshape(value.shape))
        start += value.size
    return tuple(results)


def adjacency(sources, targets, count_rows, total_rows):
    target_hot = (targets[:, None] == jnp.arange(count_rows, dtype=jnp.int32)[None, :]).astype(
        jnp.bfloat16
    )
    source_hot = (sources[:, None] == jnp.arange(total_rows, dtype=jnp.int32)[None, :]).astype(
        jnp.bfloat16
    )
    counts = lax.dot_general(
        target_hot, source_hot, (((0,), (0,)), ((), ())), preferred_element_type=jnp.float32
    )
    return counts.astype(jnp.bfloat16)


def gnn_forward(states, received, adjacent, w_message):
    extended = jnp.concatenate([states, received], axis=0)
    neighbours = jnp.dot(adjacent, extended, preferred_element_type=jnp.float32)
    counted = jnp.sum(adjacent.astype(jnp.float32), axis=1)
    inverse = 1.0 / (counted + 1.0)
    aggregate = ((states.astype(jnp.float32) + neighbours) * inverse[:, None]).astype(jnp.bfloat16)
    preact = jnp.dot(aggregate, w_message, preferred_element_type=jnp.float32)
    hidden = (states.astype(jnp.float32) + jax.nn.silu(preact)).astype(jnp.bfloat16)
    return (aggregate, preact, inverse, hidden)


def gnn_backward(upstream, aggregate, preact, inverse, adjacent, w_message):
    count_rows = aggregate.shape[0]
    up_float = upstream.astype(jnp.float32)
    sigmoid_val = jax.nn.sigmoid(preact)
    pre_grad = (up_float * sigmoid_val * (1.0 + preact * (1.0 - sigmoid_val))).astype(jnp.bfloat16)
    message_part = lax.dot_general(
        aggregate, pre_grad, (((0,), (0,)), ((), ())), preferred_element_type=jnp.float32
    )
    agg_grad = lax.dot_general(
        pre_grad, w_message, (((1,), (1,)), ((), ())), preferred_element_type=jnp.float32
    )
    term_grad = agg_grad * inverse[:, None]
    ext_grad = lax.dot_general(
        adjacent.astype(jnp.float32),
        term_grad,
        (((0,), (0,)), ((), ())),
        precision=lax.Precision.HIGHEST,
        preferred_element_type=jnp.float32,
    )
    local_grad = up_float + term_grad + ext_grad[:count_rows]
    halo_grad = ext_grad[count_rows:].astype(jnp.bfloat16)
    return (message_part, local_grad, halo_grad)


def attend(states, upstream, w_query, w_key, w_value):
    steps_all, nodes_here, width = states.shape
    head_dim = width // HEADS
    scale_factor = head_dim ** (-0.5)
    flat = states.reshape(steps_all * nodes_here, width)

    def project(weight):
        return jnp.dot(flat, weight, preferred_element_type=jnp.float32).astype(jnp.bfloat16)

    def splitter(matrix):
        return matrix.reshape(steps_all, nodes_here, HEADS, head_dim).astype(jnp.float32)

    queries = project(w_query)
    key_rows = project(w_key)
    value_rows = project(w_value)
    query_f = splitter(queries)
    key_f = splitter(key_rows)
    value_f = splitter(value_rows)
    scores = jnp.einsum("tnhd,snhd->nhts", query_f, key_f) * scale_factor
    causal = jnp.arange(steps_all)[:, None] >= jnp.arange(steps_all)[None, :]
    scores = jnp.where(causal, scores, -jnp.inf)
    highest = jnp.max(scores, axis=-1, keepdims=True)
    exponent = jnp.exp(scores - highest)
    probs = exponent / jnp.sum(exponent, axis=-1, keepdims=True)
    probs_low = probs.astype(jnp.bfloat16).astype(jnp.float32)
    up_heads = splitter(upstream)
    value_grad = jnp.einsum("nhts,tnhd->snhd", probs_low, up_heads).astype(jnp.bfloat16)
    prob_grad = jnp.einsum("tnhd,snhd->nhts", up_heads, value_f)
    score_grad = (
        probs * (prob_grad - jnp.sum(prob_grad * probs, axis=-1, keepdims=True)) * scale_factor
    ).astype(jnp.bfloat16)
    score_f = score_grad.astype(jnp.float32)
    query_grad = jnp.einsum("nhts,snhd->tnhd", score_f, key_f).astype(jnp.bfloat16)
    key_grad = jnp.einsum("nhts,tnhd->snhd", score_f, query_f).astype(jnp.bfloat16)
    query_flat = query_grad.reshape(steps_all * nodes_here, width)
    key_flat = key_grad.reshape(steps_all * nodes_here, width)
    value_flat = value_grad.reshape(steps_all * nodes_here, width)

    def weight_grad(grad_rows):
        return lax.dot_general(
            flat, grad_rows, (((0,), (0,)), ((), ())), preferred_element_type=jnp.float32
        )

    def input_grad(grad_rows, weight):
        return lax.dot_general(
            grad_rows, weight, (((1,), (1,)), ((), ())), preferred_element_type=jnp.float32
        )

    back = upstream.reshape(steps_all * nodes_here, width).astype(jnp.float32)
    back = (
        back
        + input_grad(query_flat, w_query)
        + input_grad(key_flat, w_key)
        + input_grad(value_flat, w_value)
    )
    back = back.astype(jnp.bfloat16).reshape(steps_all, nodes_here, width)
    return ((weight_grad(query_flat), weight_grad(key_flat), weight_grad(value_flat)), back)


def local(
    node_states,
    edge_source,
    edge_target,
    halo_rows,
    halo_count,
    w_message,
    w_query,
    w_key,
    w_value,
    cotangent,
):
    days_local, node_local, width = node_states.shape
    halo_slots = halo_rows.shape[1]
    live = jnp.arange(halo_slots)[None, :] < halo_count
    picked = jnp.take_along_axis(node_states, halo_rows[:, :, None], axis=1)
    sent = jnp.where(live[:, :, None], picked, jnp.zeros_like(picked))
    received = from_behind(sent, "dom", 1)

    def forward_one(items):
        adjacent = adjacency(items[2], items[3], node_local, node_local + halo_slots)
        aggregate, preact, inverse, hidden = gnn_forward(items[0], items[1], adjacent, w_message)
        return (aggregate, preact, inverse, hidden, adjacent)

    aggregate, preact, inverse, hidden, adjacent = lax.map(
        forward_one, (node_states, received, edge_source, edge_target)
    )
    node_major = lax.all_to_all(hidden, "day", split_axis=1, concat_axis=0, tiled=True)
    upstream = cotangent.reshape(cotangent.shape[0], -1, width)
    attn_grads, back = attend(node_major, upstream, w_query, w_key, w_value)
    back_days = lax.all_to_all(back, "day", split_axis=0, concat_axis=1, tiled=True)

    def backward_one(items):
        return gnn_backward(items[0], items[1], items[2], items[3], items[4], w_message)

    message_parts, local_grad, halo_grad = lax.map(
        backward_one, (back_days, aggregate, preact, inverse, adjacent)
    )
    grad_message = jnp.sum(message_parts, axis=0)
    returned = from_behind(halo_grad, "dom", -1)
    slot_hot = jnp.logical_and(
        halo_rows[:, :, None] == jnp.arange(node_local, dtype=jnp.int32)[None, None, :],
        live[:, :, None],
    ).astype(jnp.bfloat16)
    scattered = jnp.einsum("dsn,dsh->dnh", slot_hot, returned, preferred_element_type=jnp.float32)
    state_grad = local_grad + scattered
    grad_message, grad_query, grad_key, grad_value = tree_sum(
        (grad_message, attn_grads[0], attn_grads[1], attn_grads[2]), ("dom", "day")
    )
    return (state_grad, grad_message, grad_query, grad_key, grad_value)


def solution(mesh):
    return jax.shard_map(
        local,
        mesh=mesh,
        in_specs=(
            P("day", "dom", None),
            P("day", "dom"),
            P("day", "dom"),
            P("day", "dom"),
            P("day", "dom"),
            P(),
            P(),
            P(),
            P(),
            P(None, "dom", "day", None, None),
        ),
        out_specs=(P("day", "dom", None), P(), P(), P(), P()),
        check_vma=False,
    )
```

profile of v0, /device:TPU:1, one launch (start us, length us, event | category | flops | bytes accessed | tf_op | source)
XLA Modules:
  0.0 185.2 jit_solution(11964779627345640827)
XLA Ops:
  1.4 0.8 iota_compare_fusion.8
  2.1 7.0 %gather_fusion = bf16[512,256]{1,0:T(8,128)(2,1)S(1)} fusion(bf16[4,256,256]{2,1,0:T(8,128)(2,1)} %param.14, s32[512]{0:T(512)S(1)} %fusion.70), kind=kCustom, calls=%fused_computation | custom fusion | bytes 528384 | tf_op jit(solution)/shard_map/jit(take_along_axis)/gather | solution.py:173
  9.4 2.7 %collective-permute-start = (bf16[4,128,256]{2,1,0:T(8,128)(2,1)S(1)}, bf16[4,128,256]{2,1,0:T(8,128)(2,1)S(1)}, u32[]{:S(2)}, u32[]{:S(2)}) collective-permute-start(bf16[4,128,256]{2,1,0:T(8,128)(2,1)S(1)} %select_select_fusion), channel_id=1, source_target_pairs={{0,1},{1,2},{2,3},{3,4},{4,5},{5,6},{6,7},{7,0},{8,9},{9,10},{10,1... | collective-permute-start | bytes 786440 | tf_op jit(solution)/shard_map/ppermute | solution.py:12
  12.0 3.3 %collective-permute-done = bf16[4,128,256]{2,1,0:T(8,128)(2,1)S(1)} collective-permute-done((bf16[4,128,256]{2,1,0:T(8,128)(2,1)S(1)}, bf16[4,128,256]{2,1,0:T(8,128)(2,1)S(1)}, u32[]{:S(2)}, u32[]{:S(2)}) %collective-permute-start) | collective-permute-done | bytes 262176 | tf_op jit(solution)/shard_map/ppermute | solution.py:12
  15.4 14.8 %while.34 = (s32[]{:T(128)}, bf16[4,256,256]{2,1,0:T(8,128)(2,1)}, f32[4,256,256]{2,1,0:T(8,128)S(1)}, f32[4,256]{1,0:T(4,128)S(1)}, bf16[4,256,256]{2,1,0:T(8,1...) while((s32[]{:T(128)}, bf16[4,256,256]{2,1,0:T(8,128)(2,1)}, ...), condition=%wide.region_2.3_spmd.clone, body=%wide.region_0.2_spmd.sunk.clone | while | flops 287277312 | bytes 3112069 | solution.py:182
  16.2 1.0 convert_reduce_fusion.3
  17.2 0.9 bitcast_dynamic-update-slice_fusion.12
  19.9 1.0 convert_reduce_fusion.3
  20.9 0.9 bitcast_dynamic-update-slice_fusion.12
  23.6 1.0 convert_reduce_fusion.3
  24.6 0.9 bitcast_dynamic-update-slice_fusion.12
  27.2 1.0 convert_reduce_fusion.3
  28.2 0.9 bitcast_dynamic-update-slice_fusion.12
  29.4 0.8 bitcast_dynamic-update-slice_fusion.15
  30.2 1.2 copy.52
  31.4 4.6 %all-to-all-start = ((bf16[4,256,256]{2,0,1:T(4,128)(2,1)}), bf16[4,256,256]{2,0,1:T(4,128)(2,1)S(1)}, u32[]{:S(2)}, u32[]{:S(2)}) async-start(bf16[4,256,256]{2,0,1:T(4,128)(2,1)} %copy.52), calls=%async_computation | async-start | bytes 1048576 | tf_op jit(solution)/shard_map/all_to_all | solution.py:185
  36.5 12.6 %all-to-all-done = bf16[4,256,256]{2,0,1:T(4,128)(2,1)S(1)} async-done(((bf16[4,256,256]{2,0,1:T(4,128)(2,1)}), bf16[4,256,256]{2,0,1:T(4,128)(2,1)S(1)}, u32[]{:S(2)}, u32[]{:S(2)}) %all-to-all-start) | async-done | bytes 524320 | tf_op jit(solution)/shard_map/all_to_all | solution.py:185
  49.5 1.4 reshape.172
  51.2 1.4 reshape.173
  52.6 1.1 convolution_convert_fusion.3
  53.7 2.0 %reshape.174 = bf16[16,64,4,64]{3,2,1,0:T(4,128)(2,1)S(1)} reshape(bf16[1024,256]{1,0:T(8,128)(2,1)} %convolution_convert_fusion.3) | data formatting | bytes 1048576 | tf_op jit(solution)/shard_map/reshape | solution.py:109
  55.8 2.6 %fusion.52 = f32[64,4,16,16]{3,2,1,0:T(8,128)} fusion(bf16[16,64,4,64]{3,2,1,0:T(4,128)(2,1)S(1)} %reshape.174, bf16[16,64,4,64]{3,2,1,0:T(4,128)(2,1)S(1)} %reshape_reshape.4), kind=kOutput, calls=%fused_computation.91 | convolution fusion | flops 8388608 | bytes 1310720 | tf_op jit(solution)/shard_map/tnhd,snhd->nhts/dot_general | solution.py:126
  58.3 5.5 %fusion.78 = (f32[64,4,16]{2,1,0:T(4,128)}, f32[64,4,16,16]{2,3,1,0:T(8,128)}) fusion(pred[16,16]{0,1:T(8,128)(4,1)S(1)} %iota_compare_fusion.7, bf16[16,64,4,64]{3,2,1,0:T(4,128)(2,1)} %reshape.172, bf16[16,64,4,64]{3,2,1,0:T(4,128)(2,1)} %reshape.173), kind=kOutput, calls=%fused_computation.145 | convolution fusion | flops 8650767 | bytes 1327360 | tf_op jit(solution)/shard_map/sub | solution.py:121
  63.9 6.2 %fusion.50 = bf16[16,64,4,64]{3,0,2,1:T(8,128)(2,1)} fusion(f32[64,4,16,16]{3,2,1,0:T(8,128)} %fusion.52, bf16[16,64,4,64]{3,2,1,0:T(4,128)(2,1)} %reshape.173, f32[64,4,16,16]{2,3,1,0:T(8,128)} %get-tuple-element.183, f32[64,4,16]{2,1,0:T(4,128)} %get-tuple-element.182), kind=kOutput, calls=%fused_computation.78 | convolution fusion | flops 9113615 | bytes 1589248 | tf_op jit(solution)/shard_map/nhts,tnhd->snhd/dot_general | solution.py:132
  70.0 5.9 %fusion.48 = bf16[16,64,4,64]{3,0,2,1:T(8,128)(2,1)} fusion(f32[64,4,16,16]{3,2,1,0:T(8,128)} %fusion.52, bf16[16,64,4,64]{3,2,1,0:T(4,128)(2,1)S(1)} %copy-done.6, f32[64,4,16,16]{2,3,1,0:T(8,128)} %get-tuple-element.183, f32[64,4,16]{2,1,0:T(4,128)} %get-tuple-element.182), kind=kOutput, calls=%fused_computation.76 | convolution fusion | flops 9113615 | bytes 1589248 | tf_op jit(solution)/shard_map/nhts,snhd->tnhd/dot_general | solution.py:131
  75.9 3.5 %fusion.49 = bf16[16,64,4,64]{3,0,2,1:T(8,128)(2,1)} fusion(bf16[16,64,4,64]{3,2,1,0:T(4,128)(2,1)S(1)} %reshape_reshape.4, f32[64,4,16,16]{2,3,1,0:T(8,128)} %get-tuple-element.183, f32[64,4,16]{2,1,0:T(4,128)} %get-tuple-element.182), kind=kOutput, calls=%fused_computation.77 | convolution fusion | flops 8781824 | bytes 1327104 | tf_op jit(solution)/shard_map/nhts,tnhd->snhd/dot_general | solution.py:125
  79.4 2.9 %copy.63 = bf16[16,64,4,64]{1,0,3,2:T(8,128)(2,1)S(1)} copy(bf16[16,64,4,64]{3,0,2,1:T(8,128)(2,1)} %fusion.50) | data formatting | bytes 1048576 | tf_op jit(solution)/shard_map/convert_element_type | solution.py:132
  83.0 3.1 %copy.61 = bf16[16,64,4,64]{1,0,3,2:T(8,128)(2,1)S(1)} copy(bf16[16,64,4,64]{3,0,2,1:T(8,128)(2,1)} %fusion.48) | data formatting | bytes 1048576 | tf_op jit(solution)/shard_map/convert_element_type | solution.py:131
  86.9 1.1 convolution_bitcast_fusion.3
  88.3 1.1 convolution_bitcast_fusion.2
  89.7 2.9 %copy.65 = bf16[16,64,4,64]{1,0,3,2:T(8,128)(2,1)S(1)} copy(bf16[16,64,4,64]{3,0,2,1:T(8,128)(2,1)} %fusion.49) | data formatting | bytes 1048576 | tf_op jit(solution)/shard_map/convert_element_type | solution.py:125
  93.7 1.1 fusion.51
  94.9 3.5 %all-to-all-start.1 = ((bf16[16,64,256]{2,1,0:T(8,128)(2,1)}), bf16[16,64,256]{2,1,0:T(8,128)(2,1)S(1)}, u32[]{:S(2)}, u32[]{:S(2)}) async-start(bf16[16,64,256]{2,1,0:T(8,128)(2,1)} %bitcast.30), calls=%async_computation.1 | async-start | bytes 1048576 | tf_op jit(solution)/shard_map/all_to_all | solution.py:188
  98.4 0.8 copy.71
  99.5 12.0 %all-to-all-done.1 = bf16[16,64,256]{2,1,0:T(8,128)(2,1)S(1)} async-done(((bf16[16,64,256]{2,1,0:T(8,128)(2,1)}), bf16[16,64,256]{2,1,0:T(8,128)(2,1)S(1)}, u32[]{:S(2)}, u32[]{:S(2)}) %all-to-all-start.1) | async-done | bytes 524320 | tf_op jit(solution)/shard_map/all_to_all | solution.py:188
  111.8 18.2 %while.35 = (s32[]{:T(128)}, f32[4,256,256]{2,1,0:T(8,128)S(1)}, f32[4,256,256]{2,1,0:T(8,128)S(1)}, bf16[4,128,256]{2,1,0:T(8,128)(2,1)}, bf16[4,256,256]{2,1,0...) while((s32[]{:T(128)}, f32[4,256,256]{2,1,0:T(8,128)S(1)}, ...), condition=%wide.region_7.8_spmd.clone, body=%wide.region_6.7_spmd.sunk.clone | while | flops 370671616 | bytes 3479661 | solution.py:193
  111.8 1.2 convolution_multiply_fusion.3
  113.0 1.3 fusion.147
  115.0 1.3 fusion.146
  116.4 1.2 convolution_multiply_fusion.3
  117.6 1.3 fusion.147
  119.6 1.3 fusion.146
  120.9 1.2 convolution_multiply_fusion.3
  122.1 1.3 fusion.147
  124.1 1.3 fusion.146
  125.4 1.2 convolution_multiply_fusion.3
  126.6 1.3 fusion.147
  128.6 1.3 fusion.146
  131.0 2.2 %collective-permute-start.2 = (f32[131072]{0:T(1024)S(1)}, f32[131072]{0:T(1024)S(1)}, u32[]{:S(2)}, u32[]{:S(2)}) collective-permute-start(f32[131072]{0:T(1024)S(1)} %broadcast_select_fusion), channel_id=1, source_target_pairs={{0,1},{1,0},{2,3},{3,2},{4,5},{5,4},{6,7},{7,6},{8,9},{9,8},{10,11... | collective-permute-start | bytes 1572872 | tf_op jit(solution)/shard_map/ppermute | solution.py:38
  133.2 1.5 collective-permute-done.2
  134.9 2.2 %collective-permute-start.3 = (f32[65536]{0:T(1024)S(1)}, f32[65536]{0:T(1024)S(1)}, u32[]{:S(2)}, u32[]{:S(2)}) collective-permute-start(f32[65536]{0:T(1024)S(1)} %slice_select_fusion), channel_id=1, source_target_pairs={{0,2},{1,3},{2,0},{3,1},{4,6},{5,7},{6,4},{7,5},{8,10},{9,11},{10,... | collective-permute-start | bytes 786440 | tf_op jit(solution)/shard_map/ppermute | solution.py:38
  137.1 6.4 %collective-permute-done.3 = f32[65536]{0:T(1024)S(1)} collective-permute-done((f32[65536]{0:T(1024)S(1)}, f32[65536]{0:T(1024)S(1)}, u32[]{:S(2)}, u32[]{:S(2)}) %collective-permute-start.3) | collective-permute-done | bytes 262176 | tf_op jit(solution)/shard_map/ppermute | solution.py:38
  143.9 3.9 %collective-permute-done.4 = f32[32768]{0:T(1024)S(1)} collective-permute-done((f32[32768]{0:T(1024)S(1)}, f32[32768]{0:T(1024)S(1)}, u32[]{:S(2)}, u32[]{:S(2)}) %collective-permute-start.4) | collective-permute-done | bytes 131104 | tf_op jit(solution)/shard_map/ppermute | solution.py:38
  147.9 3.1 %collective-permute-done.5 = f32[16384]{0:T(1024)S(1)} collective-permute-done((f32[16384]{0:T(1024)S(1)}, f32[16384]{0:T(1024)S(1)}, u32[]{:S(2)}, u32[]{:S(2)}) %collective-permute-start.5) | collective-permute-done | bytes 65568 | tf_op jit(solution)/shard_map/ppermute | solution.py:38
  151.1 3.7 %collective-permute-done.6 = f32[8192]{0:T(1024)S(1)} collective-permute-done((f32[8192]{0:T(1024)S(1)}, f32[8192]{0:T(1024)S(1)}, u32[]{:S(2)}, u32[]{:S(2)}) %collective-permute-start.6) | collective-permute-done | bytes 32800 | tf_op jit(solution)/shard_map/ppermute | solution.py:38
  154.8 4.2 %collective-permute-done.7 = f32[8192]{0:T(1024)S(1)} collective-permute-done((f32[8192]{0:T(1024)S(1)}, f32[8192]{0:T(1024)S(1)}, u32[]{:S(2)}, u32[]{:S(2)}) %collective-permute-start.7) | collective-permute-done | bytes 32800 | tf_op jit(solution)/shard_map/ppermute | solution.py:42
  159.1 3.1 %collective-permute-done.8 = f32[16384]{0:T(1024)S(1)} collective-permute-done((f32[16384]{0:T(1024)S(1)}, f32[16384]{0:T(1024)S(1)}, u32[]{:S(2)}, u32[]{:S(2)}) %collective-permute-start.8) | collective-permute-done | bytes 65568 | tf_op jit(solution)/shard_map/ppermute | solution.py:42
  162.7 3.4 %collective-permute-done.9 = f32[32768]{0:T(1024)S(1)} collective-permute-done((f32[32768]{0:T(1024)S(1)}, f32[32768]{0:T(1024)S(1)}, u32[]{:S(2)}, u32[]{:S(2)}) %collective-permute-start.9) | collective-permute-done | bytes 131104 | tf_op jit(solution)/shard_map/ppermute | solution.py:42
  166.1 1.3 collective-permute-start.10
  167.5 7.8 %collective-permute-start.1 = (bf16[4,128,256]{2,1,0:T(8,128)(2,1)S(1)}, bf16[4,128,256]{2,1,0:T(8,128)(2,1)S(1)}, u32[]{:S(2)}, u32[]{:S(2)}) collective-permute-start(bf16[4,128,256]{2,1,0:T(8,128)(2,1)S(1)} %copy-done.13), channel_id=1, source_target_pairs={{0,7},{1,0},{2,1},{3,2},{4,3},{5,4},{6,5},{7,6},{8,15},{9,8},{10,9... | collective-permute-start | bytes 786440 | tf_op jit(solution)/shard_map/ppermute | solution.py:12
  175.3 4.9 %collective-permute-start.11 = (f32[131072]{0:T(1024)S(1)}, f32[131072]{0:T(1024)S(1)}, u32[]{:S(2)}, u32[]{:S(2)}) collective-permute-start(f32[131072]{0:T(1024)S(1)} %maximum_select_fusion.2), channel_id=1, source_target_pairs={{0,1},{1,0},{2,3},{3,2},{4,5},{5,4},{6,7},{7,6},{8,9},{9,8},{10,11... | collective-permute-start | bytes 1572872 | tf_op jit(solution)/shard_map/ppermute | solution.py:42
  180.2 2.0 %collective-permute-done.1 = bf16[4,128,256]{2,1,0:T(8,128)(2,1)S(1)} collective-permute-done((bf16[4,128,256]{2,1,0:T(8,128)(2,1)S(1)}, bf16[4,128,256]{2,1,0:T(8,128)(2,1)S(1)}, u32[]{:S(2)}, u32[]{:S(2)}) %collective-permute-start.1) | collective-permute-done | bytes 262176 | tf_op jit(solution)/shard_map/ppermute | solution.py:12
  182.2 1.5 convolution_add_fusion.4
  184.2 1.0 fusion.77
  (133 shorter events, 17.9 us)
Async XLA Ops:
  0.6 50.3 %copy-start = (bf16[256,256]{1,0:T(8,128)(2,1)S(1)}, bf16[256,256]{1,0:T(8,128)(2,1)}, u32[]{:S(2)}) copy-start(bf16[256,256]{1,0:T(8,128)(2,1)} %param.20) | copy-start | bytes 393220
  2.1 13.3 %copy-start.1 = (bf16[4,256,256]{2,1,0:T(8,128)(2,1)S(1)}, bf16[4,256,256]{2,1,0:T(8,128)(2,1)}, u32[]{:S(2)}) copy-start(bf16[4,256,256]{2,1,0:T(8,128)(2,1)} %param.14) | copy-start | bytes 1572868
  2.1 13.3 %copy-start.2 = (bf16[256,256]{1,0:T(8,128)(2,1)S(1)}, bf16[256,256]{1,0:T(8,128)(2,1)}, u32[]{:S(2)}) copy-start(bf16[256,256]{1,0:T(8,128)(2,1)} %param.19) | copy-start | bytes 393220
  9.4 6.0 %collective-permute-start = (bf16[4,128,256]{2,1,0:T(8,128)(2,1)S(1)}, bf16[4,128,256]{2,1,0:T(8,128)(2,1)S(1)}, u32[]{:S(2)}, u32[]{:S(2)}) collective-permute-start(bf16[4,128,256]{2,1,0:T(8,128)(2,1)S(1)} %select_select_fusion), channel_id=1, source_target_pairs={{0,1},{1,2},{2,3},{3,4},{4,5},{5,6},{6,7},{7,0},{8,9},{9,10},{10,1... | collective-permute-start | bytes 786440 | tf_op jit(solution)/shard_map/ppermute | solution.py:12
  30.2 5.8 %copy-start.7 = (f32[4,256,256]{2,1,0:T(8,128)}, f32[4,256,256]{2,1,0:T(8,128)S(1)}, u32[]{:S(2)}) copy-start(f32[4,256,256]{2,1,0:T(8,128)S(1)} %get-tuple-element.424) | copy-start | bytes 3145732
  30.2 5.8 %copy-start.3 = (bf16[16,1,1,64,256]{4,3,2,1,0:T(8,128)(2,1)S(1)}, bf16[16,1,1,64,256]{4,3,2,1,0:T(8,128)(2,1)}, u32[]{:S(2)}) copy-start(bf16[16,1,1,64,256]{4,3,2,1,0:T(8,128)(2,1)} %param.23) | copy-start | bytes 1572868
  31.4 17.7 %all-to-all-start = ((bf16[4,256,256]{2,0,1:T(4,128)(2,1)}), bf16[4,256,256]{2,0,1:T(4,128)(2,1)S(1)}, u32[]{:S(2)}, u32[]{:S(2)}) async-start(bf16[4,256,256]{2,0,1:T(4,128)(2,1)} %copy.52), calls=%async_computation | async-start | bytes 1048576 | tf_op jit(solution)/shard_map/all_to_all | solution.py:185
  36.0 13.2 %copy-start.10 = (bf16[256,256]{1,0:T(8,128)(2,1)S(1)}, bf16[256,256]{1,0:T(8,128)(2,1)}, u32[]{:S(2)}) copy-start(bf16[256,256]{1,0:T(8,128)(2,1)} %param.21) | copy-start | bytes 393220
  49.5 3.1 %copy-start.9 = (bf16[256,256]{1,0:T(8,128)(2,1)S(1)}, bf16[256,256]{1,0:T(8,128)(2,1)}, u32[]{:S(2)}) copy-start(bf16[256,256]{1,0:T(8,128)(2,1)} %param.22) | copy-start | bytes 393220
  63.9 6.2 %copy-start.6 = (bf16[16,64,4,64]{3,2,1,0:T(4,128)(2,1)S(1)}, bf16[16,64,4,64]{3,2,1,0:T(4,128)(2,1)}, u32[]{:S(2)}) copy-start(bf16[16,64,4,64]{3,2,1,0:T(4,128)(2,1)} %reshape.172) | copy-start | bytes 1572868
  87.9 1.4 copy-start.11
  93.3 5.0 %copy-start.4 = (f32[32,2,8,128]{3,2,1,0:T(8,128)S(1)}, f32[32,2,8,128]{3,2,1,0:T(8,128)}, u32[]{:S(2)}) copy-start(f32[32,2,8,128]{3,2,1,0:T(8,128)} %convolution_bitcast_fusion.3) | copy-start | bytes 786436
  93.7 5.5 %copy-start.5 = (f32[32,2,8,128]{3,2,1,0:T(8,128)S(1)}, f32[32,2,8,128]{3,2,1,0:T(8,128)}, u32[]{:S(2)}) copy-start(f32[32,2,8,128]{3,2,1,0:T(8,128)} %convolution_bitcast_fusion.2) | copy-start | bytes 786436
  94.9 16.7 %all-to-all-start.1 = ((bf16[16,64,256]{2,1,0:T(8,128)(2,1)}), bf16[16,64,256]{2,1,0:T(8,128)(2,1)S(1)}, u32[]{:S(2)}, u32[]{:S(2)}) async-start(bf16[16,64,256]{2,1,0:T(8,128)(2,1)} %bitcast.30), calls=%async_computation.1 | async-start | bytes 1048576 | tf_op jit(solution)/shard_map/all_to_all | solution.py:188
  129.9 1.0 copy-start.8
  131.0 3.8 %collective-permute-start.2 = (f32[131072]{0:T(1024)S(1)}, f32[131072]{0:T(1024)S(1)}, u32[]{:S(2)}, u32[]{:S(2)}) collective-permute-start(f32[131072]{0:T(1024)S(1)} %broadcast_select_fusion), channel_id=1, source_target_pairs={{0,1},{1,0},{2,3},{3,2},{4,5},{5,4},{6,7},{7,6},{8,9},{9,8},{10,11... | collective-permute-start | bytes 1572872 | tf_op jit(solution)/shard_map/ppermute | solution.py:38
  134.9 32.6 %copy-start.13 = (bf16[4,128,256]{2,1,0:T(8,128)(2,1)S(1)}, bf16[4,128,256]{2,1,0:T(8,128)(2,1)}, u32[]{:S(2)}) copy-start(bf16[4,128,256]{2,1,0:T(8,128)(2,1)} %get-tuple-element.126) | copy-start | bytes 786436
  134.9 8.6 %collective-permute-start.3 = (f32[65536]{0:T(1024)S(1)}, f32[65536]{0:T(1024)S(1)}, u32[]{:S(2)}, u32[]{:S(2)}) collective-permute-start(f32[65536]{0:T(1024)S(1)} %slice_select_fusion), channel_id=1, source_target_pairs={{0,2},{1,3},{2,0},{3,1},{4,6},{5,7},{6,4},{7,5},{8,10},{9,11},{10,... | collective-permute-start | bytes 786440 | tf_op jit(solution)/shard_map/ppermute | solution.py:38
  137.1 45.1 %copy-start.12 = (s32[4,128]{1,0:T(4,128)S(1)}, s32[4,128]{1,0:T(4,128)}, u32[]{:S(2)}) copy-start(s32[4,128]{1,0:T(4,128)} %param.17) | copy-start | bytes 6148
  143.6 4.2 %collective-permute-start.4 = (f32[32768]{0:T(1024)S(1)}, f32[32768]{0:T(1024)S(1)}, u32[]{:S(2)}, u32[]{:S(2)}) collective-permute-start(f32[32768]{0:T(1024)S(1)} %slice_select_fusion.1), channel_id=1, source_target_pairs={{0,4},{1,5},{2,6},{3,7},{4,0},{5,1},{6,2},{7,3},{8,12},{9,13},{10,... | collective-permute-start | bytes 393224 | tf_op jit(solution)/shard_map/ppermute | solution.py:38
  147.8 3.2 %collective-permute-start.5 = (f32[16384]{0:T(1024)S(1)}, f32[16384]{0:T(1024)S(1)}, u32[]{:S(2)}, u32[]{:S(2)}) collective-permute-start(f32[16384]{0:T(1024)S(1)} %slice_select_fusion.2), channel_id=1, source_target_pairs={{0,8},{8,0},{16,24},{24,16},{1,9},{9,1},{17,25},{25,17},{2,10},{10... | collective-permute-start | bytes 196616 | tf_op jit(solution)/shard_map/ppermute | solution.py:38
  151.0 3.8 %collective-permute-start.6 = (f32[8192]{0:T(1024)S(1)}, f32[8192]{0:T(1024)S(1)}, u32[]{:S(2)}, u32[]{:S(2)}) collective-permute-start(f32[8192]{0:T(1024)S(1)} %slice_select_fusion.3), channel_id=1, source_target_pairs={{0,16},{8,24},{16,0},{24,8},{1,17},{9,25},{17,1},{25,9},{2,18},{10... | collective-permute-start | bytes 98312 | tf_op jit(solution)/shard_map/ppermute | solution.py:38
  154.8 4.2 %collective-permute-start.7 = (f32[8192]{0:T(1024)S(1)}, f32[8192]{0:T(1024)S(1)}, u32[]{:S(2)}, u32[]{:S(2)}) collective-permute-start(f32[8192]{0:T(1024)S(1)} %select_add_fusion.4), channel_id=1, source_target_pairs={{0,16},{8,24},{16,0},{24,8},{1,17},{9,25},{17,1},{25,9},{2,18},{10... | collective-permute-start | bytes 98312 | tf_op jit(solution)/shard_map/ppermute | solution.py:42
  159.0 3.2 %collective-permute-start.8 = (f32[16384]{0:T(1024)S(1)}, f32[16384]{0:T(1024)S(1)}, u32[]{:S(2)}, u32[]{:S(2)}) collective-permute-start(f32[16384]{0:T(1024)S(1)} %maximum_select_fusion.7), channel_id=1, source_target_pairs={{0,8},{8,0},{16,24},{24,16},{1,9},{9,1},{17,25},{25,17},{2,10},{10... | collective-permute-start | bytes 196616 | tf_op jit(solution)/shard_map/ppermute | solution.py:42
  162.2 3.9 %collective-permute-start.9 = (f32[32768]{0:T(1024)S(1)}, f32[32768]{0:T(1024)S(1)}, u32[]{:S(2)}, u32[]{:S(2)}) collective-permute-start(f32[32768]{0:T(1024)S(1)} %maximum_select_fusion.6), channel_id=1, source_target_pairs={{0,4},{1,5},{2,6},{3,7},{4,0},{5,1},{6,2},{7,3},{8,12},{9,13},{10,... | collective-permute-start | bytes 393224 | tf_op jit(solution)/shard_map/ppermute | solution.py:42
  166.1 9.2 %collective-permute-start.10 = (f32[65536]{0:T(1024)S(1)}, f32[65536]{0:T(1024)S(1)}, u32[]{:S(2)}, u32[]{:S(2)}) collective-permute-start(f32[65536]{0:T(1024)S(1)} %maximum_select_fusion.4), channel_id=1, source_target_pairs={{0,2},{1,3},{2,0},{3,1},{4,6},{5,7},{6,4},{7,5},{8,10},{9,11},{10,... | collective-permute-start | bytes 786440 | tf_op jit(solution)/shard_map/ppermute | solution.py:42
  167.5 14.7 %collective-permute-start.1 = (bf16[4,128,256]{2,1,0:T(8,128)(2,1)S(1)}, bf16[4,128,256]{2,1,0:T(8,128)(2,1)S(1)}, u32[]{:S(2)}, u32[]{:S(2)}) collective-permute-start(bf16[4,128,256]{2,1,0:T(8,128)(2,1)S(1)} %copy-done.13), channel_id=1, source_target_pairs={{0,7},{1,0},{2,1},{3,2},{4,3},{5,4},{6,5},{7,6},{8,15},{9,8},{10,9... | collective-permute-start | bytes 786440 | tf_op jit(solution)/shard_map/ppermute | solution.py:12
  175.3 8.6 %collective-permute-start.11 = (f32[131072]{0:T(1024)S(1)}, f32[131072]{0:T(1024)S(1)}, u32[]{:S(2)}, u32[]{:S(2)}) collective-permute-start(f32[131072]{0:T(1024)S(1)} %maximum_select_fusion.2), channel_id=1, source_target_pairs={{0,1},{1,0},{2,3},{3,2},{4,5},{5,4},{6,7},{7,6},{8,9},{9,8},{10,11... | collective-permute-start | bytes 1572872 | tf_op jit(solution)/shard_map/ppermute | solution.py:42
where the time goes:
time: 186 us; the launch traced here: 185 us
  waiting for transfers between devices  59.3 us (32%)
  matrix products  54.4 us (29%)
  local copies, waits for them, and re-layouts  36.9 us (20%)
  starting transfers between devices  30.2 us (16%)
  other arithmetic  2.89 us (2%)
    ppermute x5, waiting for transfers between devices, tree_sum(): flat = keep + lax.ppermute(send, axis, pairs)  18.6 us
    all_to_all x1, waiting for transfers between devices, local(): lax.all_to_all(hidden, 'day', split_axis=1, concat_axis=0, tiled=True)  12.6 us
    all_to_all x1, waiting for transfers between devices, local(): lax.all_to_all(back, 'day', split_axis=0, concat_axis=1, tiled=True)  12 us
    ppermute x5, waiting for transfers between devices, tree_sum(): other = lax.ppermute(flat, axis, pairs)  10.7 us
    ppermute x2, starting transfers between devices, from_behind(): return lax.ppermute(value, axis, pairs)  10.5 us
    gather x1, local copies, waits for them, and re-layouts, local(): picked = jnp.take_along_axis(node_states, halo_rows[:, :, None], axis=1)  7 us
    ppermute x5, starting transfers between devices, tree_sum(): other = lax.ppermute(flat, axis, pairs)  6.72 us
    dot_general x1, matrix products, attend(): jnp.einsum('nhts,tnhd->snhd', score_f, query_f).astype(jnp.bfloat16)  6.16 us
  transfers between devices with their start and end apart: 14, of which 12 were waited for; matrix products, arithmetic and copies ran while one was open for 2% of the time, Pallas kernels for 0%

commit v1 on v0

--- a/solution.py
+++ b/solution.py
@@ -4,6 +4,18 @@
 from jax.sharding import PartitionSpec as P
 
 HEADS = 4
+
+
+def in_blocks(array, dim, size):
+    dims = array.shape
+    blocks = array.reshape(*dims[:dim], size, dims[dim] // size, *dims[dim + 1 :])
+    return jnp.moveaxis(blocks, dim, 0)
+
+
+def laid_out(tiles, dim):
+    tiles = jnp.moveaxis(tiles, 0, dim)
+    dims = tiles.shape
+    return tiles.reshape(*dims[:dim], dims[dim] * dims[dim + 1], *dims[dim + 2 :])
 
 
 def from_behind(value, axis, steps):
@@ -182,7 +194,14 @@
     aggregate, preact, inverse, hidden, adjacent = lax.map(
         forward_one, (node_states, received, edge_source, edge_target)
     )
-    node_major = lax.all_to_all(hidden, "day", split_axis=1, concat_axis=0, tiled=True)
+    count_2, place = (lax.axis_size("day"), lax.axis_index("day"))
+    blocks = in_blocks(hidden, 1, count_2)
+    done = [blocks[place]]
+    for lap in range(1, count_2):
+        sent_2 = blocks[(place + lap) % count_2]
+        done.append(lax.ppermute(sent_2, "day", [(i, (i + lap) % count_2) for i in range(count_2)]))
+    blocks = jnp.stack(done)[(place - jnp.arange(count_2)) % count_2]
+    node_major = laid_out(blocks, 0)
     upstream = cotangent.reshape(cotangent.shape[0], -1, width)
     attn_grads, back = attend(node_major, upstream, w_query, w_key, w_value)
     back_days = lax.all_to_all(back, "day", split_axis=0, concat_axis=1, tiled=True)

time: 186 us -> 176 us (0.946)
  waiting for transfers between devices: 59.3 us -> 52.4 us
  matrix products: 54.4 us -> 51.6 us
  local copies, waits for them, and re-layouts: 36.9 us -> 34.5 us
  starting transfers between devices: 30.2 us -> 32.5 us
    all_to_all x1 -> x0, waiting for transfers between devices: 12.6 us -> none  [local(): lax.all_to_all(hidden, 'day', split_axis=1, concat_axis=0, tiled=True)]
    ppermute x0 -> x3, waiting for transfers between devices: none -> 7.79 us  [local(): lax.ppermute(sent_2, 'day', [(i, (i + lap) % count_2) for i in range(coun...]
    ppermute x0 -> x3, starting transfers between devices: none -> 4.72 us  [local(): lax.ppermute(sent_2, 'day', [(i, (i + lap) % count_2) for i in range(coun...]
    all_to_all x1 -> x0, starting transfers between devices: 4.59 us -> none  [local(): lax.all_to_all(hidden, 'day', split_axis=1, concat_axis=0, tiled=True)]
    ppermute x5, waiting for transfers between devices: 18.6 us -> 16.7 us  [tree_sum(): flat = keep + lax.ppermute(send, axis, pairs)]
  transfers between devices with their start and end apart: 14 -> 16, of which waited for: 12 -> 13; matrix products, arithmetic and copies ran while one was open for 2% -> 2% of each run, Pallas kernels for 0% -> 0%
where the time goes in v1:
time: 176 us; the launch traced here: 175 us
  waiting for transfers between devices  52.4 us (30%)
  matrix products  51.6 us (29%)
  local copies, waits for them, and re-layouts  34.5 us (20%)
  starting transfers between devices  32.5 us (18%)
  other arithmetic  2.97 us (2%)
    ppermute x5, waiting for transfers between devices, tree_sum(): flat = keep + lax.ppermute(send, axis, pairs)  16.7 us
    all_to_all x1, waiting for transfers between devices, local(): lax.all_to_all(back, 'day', split_axis=0, concat_axis=1, tiled=True)  12.8 us
    ppermute x2, starting transfers between devices, from_behind(): return lax.ppermute(value, axis, pairs)  10.5 us
    ppermute x5, waiting for transfers between devices, tree_sum(): other = lax.ppermute(flat, axis, pairs)  9.8 us
    ppermute x5, starting transfers between devices, tree_sum(): other = lax.ppermute(flat, axis, pairs)  8.13 us
    ppermute x3, waiting for transfers between devices, local(): lax.ppermute(sent_2, 'day', [(i, (i + lap) % count_2) for i in range(coun...  7.79 us
    gather x1, local copies, waits for them, and re-layouts, local(): picked = jnp.take_along_axis(node_states, halo_rows[:, :, None], axis=1)  7 us
    dot_general x1, matrix products, attend(): jnp.einsum('nhts,tnhd->snhd', score_f, query_f).astype(jnp.bfloat16)  6.13 us
  transfers between devices with their start and end apart: 16, of which 13 were waited for; matrix products, arithmetic and copies ran while one was open for 2% of the time, Pallas kernels for 0%

profile of v1, /device:TPU:1, one launch (start us, length us, event | category | flops | bytes accessed | tf_op | source)
XLA Modules:
  0.0 175.5 jit_solution(10363302863783780085)
XLA Ops:
  2.1 7.0 %gather_fusion.1 = bf16[512,256]{1,0:T(8,128)(2,1)S(1)} fusion(bf16[4,256,256]{2,1,0:T(8,128)(2,1)} %param.14, s32[512]{0:T(512)S(1)} %fusion.70), kind=kCustom, calls=%fused_computation.1 | custom fusion | bytes 528384 | tf_op jit(solution)/shard_map/jit(take_along_axis)/gather | solution.py:185
  9.4 2.7 %collective-permute-start = (bf16[4,128,256]{2,1,0:T(8,128)(2,1)S(1)}, bf16[4,128,256]{2,1,0:T(8,128)(2,1)S(1)}, u32[]{:S(2)}, u32[]{:S(2)}) collective-permute-start(bf16[4,128,256]{2,1,0:T(8,128)(2,1)S(1)} %select_select_fusion), channel_id=1, source_target_pairs={{0,1},{1,2},{2,3},{3,4},{4,5},{5,6},{6,7},{7,0},{8,9},{9,10},{10,1... | collective-permute-start | bytes 786440 | tf_op jit(solution)/shard_map/ppermute | solution.py:24
  12.0 3.3 %collective-permute-done = bf16[4,128,256]{2,1,0:T(8,128)(2,1)S(1)} collective-permute-done((bf16[4,128,256]{2,1,0:T(8,128)(2,1)S(1)}, bf16[4,128,256]{2,1,0:T(8,128)(2,1)S(1)}, u32[]{:S(2)}, u32[]{:S(2)}) %collective-permute-start) | collective-permute-done | bytes 262176 | tf_op jit(solution)/shard_map/ppermute | solution.py:24
  15.4 14.8 %while.34 = (s32[]{:T(128)}, bf16[4,256,256]{2,1,0:T(8,128)(2,1)}, f32[4,256,256]{2,1,0:T(8,128)S(1)}, f32[4,256]{1,0:T(4,128)S(1)}, bf16[4,256,256]{2,1,0:T(8,1...) while((s32[]{:T(128)}, bf16[4,256,256]{2,1,0:T(8,128)(2,1)}, ...), condition=%wide.region_2.3_spmd.clone, body=%wide.region_0.2_spmd.sunk.clone | while | flops 287277312 | bytes 3112069 | solution.py:194
  15.5 0.8 constant_dynamic-slice_fusion.7
  16.3 1.0 convert_reduce_fusion.3
  17.3 0.9 bitcast_dynamic-update-slice_fusion.12
  19.9 1.0 convert_reduce_fusion.3
  21.0 0.9 bitcast_dynamic-update-slice_fusion.12
  23.6 1.0 convert_reduce_fusion.3
  24.7 0.9 bitcast_dynamic-update-slice_fusion.12
  27.3 1.0 convert_reduce_fusion.3
  28.3 0.9 bitcast_dynamic-update-slice_fusion.12
  30.3 1.3 collective-permute-start.1
  31.7 2.3 %collective-permute-start.2 = (bf16[4,64,256]{2,1,0:T(8,128)(2,1)S(1)}, bf16[4,64,256]{2,1,0:T(8,128)(2,1)S(1)}, u32[]{:S(2)}, u32[]{:S(2)}) collective-permute-start(bf16[4,64,256]{2,1,0:T(8,128)(2,1)S(1)} %get-tuple-element.184), channel_id=1, source_target_pairs={{0,16},{8,24},{16,0},{24,8},{1,17},{9,25},{17,1},{25,9},{2,18},{10... | collective-permute-start | bytes 393224 | tf_op jit(solution)/shard_map/ppermute | solution.py:202
  34.0 1.1 collective-permute-start.3
  36.2 7.2 %collective-permute-done.2 = bf16[4,64,256]{2,1,0:T(8,128)(2,1)S(1)} collective-permute-done((bf16[4,64,256]{2,1,0:T(8,128)(2,1)S(1)}, bf16[4,64,256]{2,1,0:T(8,128)(2,1)S(1)}, u32[]{:S(2)}, u32[]{:S(2)}) %collective-permute-start.2) | collective-permute-done | bytes 131104 | tf_op jit(solution)/shard_map/ppermute | solution.py:202
  44.3 1.4 reshape.227
  46.0 1.5 reshape.228
  48.2 2.6 %fusion.52 = f32[64,4,16,16]{3,2,1,0:T(8,128)} fusion(bf16[16,64,4,64]{3,2,1,0:T(4,128)(2,1)S(1)} %reshape.229, bf16[16,64,4,64]{3,2,1,0:T(4,128)(2,1)S(1)} %reshape_reshape.8), kind=kOutput, calls=%fused_computation.92 | convolution fusion | flops 8388608 | bytes 1310720 | tf_op jit(solution)/shard_map/tnhd,snhd->nhts/dot_general | solution.py:138
  50.8 4.9 %fusion.80 = (f32[64,4,16]{2,1,0:T(4,128)S(1)}, f32[64,4,16,16]{2,3,1,0:T(8,128)}) fusion(pred[16,16]{0,1:T(8,128)(4,1)S(1)} %iota_compare_fusion.7, bf16[16,64,4,64]{3,2,1,0:T(4,128)(2,1)} %reshape.227, bf16[16,64,4,64]{3,2,1,0:T(4,128)(2,1)} %reshape.228), kind=kOutput, calls=%fused_computation.158 | convolution fusion | flops 8650767 | bytes 1327360 | tf_op jit(solution)/shard_map/sub | solution.py:133
  55.7 3.5 %fusion.49 = bf16[16,64,4,64]{3,0,2,1:T(8,128)(2,1)} fusion(bf16[16,64,4,64]{3,2,1,0:T(4,128)(2,1)S(1)} %reshape_reshape.8, f32[64,4,16,16]{2,3,1,0:T(8,128)} %get-tuple-element.187, f32[64,4,16]{2,1,0:T(4,128)S(1)} %get-tuple-element.186), kind=kOutput, calls=%fused_computation.78 | convolution fusion | flops 8781824 | bytes 1327104 | tf_op jit(solution)/shard_map/nhts,tnhd->snhd/dot_general | solution.py:137
  59.1 6.1 %fusion.50 = bf16[16,64,4,64]{3,0,2,1:T(8,128)(2,1)} fusion(f32[64,4,16,16]{3,2,1,0:T(8,128)} %fusion.52, bf16[16,64,4,64]{3,2,1,0:T(4,128)(2,1)} %reshape.228, f32[64,4,16,16]{2,3,1,0:T(8,128)} %get-tuple-element.187, f32[64,4,16]{2,1,0:T(4,128)S(1)} %get-tuple-element.186), kind=kOutput, calls=%fused_computation.79 | convolution fusion | flops 9113615 | bytes 1589248 | tf_op jit(solution)/shard_map/nhts,tnhd->snhd/dot_general | solution.py:144
  65.3 4.9 %fusion.48 = bf16[16,64,4,64]{3,0,2,1:T(8,128)(2,1)} fusion(f32[64,4,16,16]{3,2,1,0:T(8,128)S(1)} %copy-done.4, bf16[16,64,4,64]{3,2,1,0:T(4,128)(2,1)} %reshape.227, f32[64,4,16,16]{2,3,1,0:T(8,128)} %get-tuple-element.187, f32[64,4,16]{2,1,0:T(4,128)S(1)} %get-tuple-element.186), kind=kOutput, calls=%fused_computation.77 | convolution fusion | flops 9113615 | bytes 1589248 | tf_op jit(solution)/shard_map/nhts,snhd->tnhd/dot_general | solution.py:143
  70.2 2.9 %copy.35 = bf16[16,64,4,64]{1,0,3,2:T(8,128)(2,1)S(1)} copy(bf16[16,64,4,64]{3,0,2,1:T(8,128)(2,1)} %fusion.49) | data formatting | bytes 1048576 | tf_op jit(solution)/shard_map/convert_element_type | solution.py:137
  73.8 2.9 %copy.33 = bf16[16,64,4,64]{1,0,3,2:T(8,128)(2,1)S(1)} copy(bf16[16,64,4,64]{3,0,2,1:T(8,128)(2,1)} %fusion.50) | data formatting | bytes 1048576 | tf_op jit(solution)/shard_map/convert_element_type | solution.py:144
  77.4 2.9 %copy.31 = bf16[16,64,4,64]{1,0,3,2:T(8,128)(2,1)S(1)} copy(bf16[16,64,4,64]{3,0,2,1:T(8,128)(2,1)} %fusion.48) | data formatting | bytes 1048576 | tf_op jit(solution)/shard_map/convert_element_type | solution.py:143
  81.4 1.4 convolution_add_fusion.3
  83.9 1.1 fusion.51
  85.1 4.3 %all-to-all-start = ((bf16[16,64,256]{2,1,0:T(8,128)(2,1)}), bf16[16,64,256]{2,1,0:T(8,128)(2,1)S(1)}, u32[]{:S(2)}, u32[]{:S(2)}) async-start(bf16[16,64,256]{2,1,0:T(8,128)(2,1)} %bitcast.37), calls=%async_computation | async-start | bytes 1048576 | tf_op jit(solution)/shard_map/all_to_all | solution.py:207
  89.4 0.8 copy.41
  90.6 12.8 %all-to-all-done = bf16[16,64,256]{2,1,0:T(8,128)(2,1)S(1)} async-done(((bf16[16,64,256]{2,1,0:T(8,128)(2,1)}), bf16[16,64,256]{2,1,0:T(8,128)(2,1)S(1)}, u32[]{:S(2)}, u32[]{:S(2)}) %all-to-all-start) | async-done | bytes 524320 | tf_op jit(solution)/shard_map/all_to_all | solution.py:207
  103.6 18.2 %while.35 = (s32[]{:T(128)}, f32[4,256,256]{2,1,0:T(8,128)S(1)}, f32[4,256,256]{2,1,0:T(8,128)S(1)}, bf16[4,128,256]{2,1,0:T(8,128)(2,1)}, bf16[4,256,256]{2,1,0...) while((s32[]{:T(128)}, f32[4,256,256]{2,1,0:T(8,128)S(1)}, ...), condition=%wide.region_7.8_spmd.clone, body=%wide.region_6.7_spmd.sunk.clone | while | flops 370671616 | bytes 3479661 | solution.py:212
  103.7 1.2 convolution_multiply_fusion.3
  104.9 1.3 fusion.149
  106.9 1.3 fusion.148
  108.2 1.2 convolution_multiply_fusion.3
  109.4 1.3 fusion.149
  111.4 1.3 fusion.148
  112.7 1.2 convolution_multiply_fusion.3
  114.0 1.3 fusion.149
  116.0 1.3 fusion.148
  117.3 1.2 convolution_multiply_fusion.3
  118.5 1.3 fusion.149
  120.5 1.3 fusion.148
  122.8 1.5 collective-permute-start.5
  124.4 1.5 collective-permute-done.5
  126.0 1.2 collective-permute-start.6
  127.3 6.3 %collective-permute-done.6 = f32[65536]{0:T(1024)S(1)} collective-permute-done((f32[65536]{0:T(1024)S(1)}, f32[65536]{0:T(1024)S(1)}, u32[]{:S(2)}, u32[]{:S(2)}) %collective-permute-start.6) | collective-permute-done | bytes 262176 | tf_op jit(solution)/shard_map/ppermute | solution.py:50
  133.7 1.2 collective-permute-start.7
  134.9 2.7 %collective-permute-done.7 = f32[32768]{0:T(1024)S(1)} collective-permute-done((f32[32768]{0:T(1024)S(1)}, f32[32768]{0:T(1024)S(1)}, u32[]{:S(2)}, u32[]{:S(2)}) %collective-permute-start.7) | collective-permute-done | bytes 131104 | tf_op jit(solution)/shard_map/ppermute | solution.py:50
  137.7 3.1 %collective-permute-done.8 = f32[16384]{0:T(1024)S(1)} collective-permute-done((f32[16384]{0:T(1024)S(1)}, f32[16384]{0:T(1024)S(1)}, u32[]{:S(2)}, u32[]{:S(2)}) %collective-permute-start.8) | collective-permute-done | bytes 65568 | tf_op jit(solution)/shard_map/ppermute | solution.py:50
  140.8 0.8 collective-permute-start.9
  141.6 3.0 %collective-permute-done.9 = f32[8192]{0:T(1024)S(1)} collective-permute-done((f32[8192]{0:T(1024)S(1)}, f32[8192]{0:T(1024)S(1)}, u32[]{:S(2)}, u32[]{:S(2)}) %collective-permute-start.9) | collective-permute-done | bytes 32800 | tf_op jit(solution)/shard_map/ppermute | solution.py:50
  145.3 4.0 %collective-permute-done.10 = f32[8192]{0:T(1024)S(1)} collective-permute-done((f32[8192]{0:T(1024)S(1)}, f32[8192]{0:T(1024)S(1)}, u32[]{:S(2)}, u32[]{:S(2)}) %collective-permute-start.10) | collective-permute-done | bytes 32800 | tf_op jit(solution)/shard_map/ppermute | solution.py:54
  149.4 3.1 %collective-permute-done.11 = f32[16384]{0:T(1024)S(1)} collective-permute-done((f32[16384]{0:T(1024)S(1)}, f32[16384]{0:T(1024)S(1)}, u32[]{:S(2)}, u32[]{:S(2)}) %collective-permute-start.11) | collective-permute-done | bytes 65568 | tf_op jit(solution)/shard_map/ppermute | solution.py:54
  152.5 1.2 collective-permute-start.12
  153.7 2.7 %collective-permute-done.12 = f32[32768]{0:T(1024)S(1)} collective-permute-done((f32[32768]{0:T(1024)S(1)}, f32[32768]{0:T(1024)S(1)}, u32[]{:S(2)}, u32[]{:S(2)}) %collective-permute-start.12) | collective-permute-done | bytes 131104 | tf_op jit(solution)/shard_map/ppermute | solution.py:54
  156.4 1.2 collective-permute-start.13
  157.6 7.8 %collective-permute-start.4 = (bf16[4,128,256]{2,1,0:T(8,128)(2,1)S(1)}, bf16[4,128,256]{2,1,0:T(8,128)(2,1)S(1)}, u32[]{:S(2)}, u32[]{:S(2)}) collective-permute-start(bf16[4,128,256]{2,1,0:T(8,128)(2,1)S(1)} %copy-done.11), channel_id=1, source_target_pairs={{0,7},{1,0},{2,1},{3,2},{4,3},{5,4},{6,5},{7,6},{8,15},{9,8},{10,9... | collective-permute-start | bytes 786440 | tf_op jit(solution)/shard_map/ppermute | solution.py:24
  165.5 5.0 %collective-permute-start.14 = (f32[131072]{0:T(1024)S(1)}, f32[131072]{0:T(1024)S(1)}, u32[]{:S(2)}, u32[]{:S(2)}) collective-permute-start(f32[131072]{0:T(1024)S(1)} %maximum_select_fusion.2), channel_id=1, source_target_pairs={{0,1},{1,0},{2,3},{3,2},{4,5},{5,4},{6,7},{7,6},{8,9},{9,8},{10,11... | collective-permute-start | bytes 1572872 | tf_op jit(solution)/shard_map/ppermute | solution.py:54
  170.5 2.0 %collective-permute-done.4 = bf16[4,128,256]{2,1,0:T(8,128)(2,1)S(1)} collective-permute-done((bf16[4,128,256]{2,1,0:T(8,128)(2,1)S(1)}, bf16[4,128,256]{2,1,0:T(8,128)(2,1)S(1)}, u32[]{:S(2)}, u32[]{:S(2)}) %collective-permute-start.4) | collective-permute-done | bytes 262176 | tf_op jit(solution)/shard_map/ppermute | solution.py:24
  172.5 1.5 convolution_add_fusion.4
  174.5 1.0 fusion.79
  (135 shorter events, 20.7 us)
Async XLA Ops:
  0.6 45.1 %copy-start = (bf16[256,256]{1,0:T(8,128)(2,1)S(1)}, bf16[256,256]{1,0:T(8,128)(2,1)}, u32[]{:S(2)}) copy-start(bf16[256,256]{1,0:T(8,128)(2,1)} %param.20) | copy-start | bytes 393220
  2.1 13.3 %copy-start.1 = (bf16[4,256,256]{2,1,0:T(8,128)(2,1)S(1)}, bf16[4,256,256]{2,1,0:T(8,128)(2,1)}, u32[]{:S(2)}) copy-start(bf16[4,256,256]{2,1,0:T(8,128)(2,1)} %param.14) | copy-start | bytes 1572868
  2.1 13.3 %copy-start.2 = (bf16[256,256]{1,0:T(8,128)(2,1)S(1)}, bf16[256,256]{1,0:T(8,128)(2,1)}, u32[]{:S(2)}) copy-start(bf16[256,256]{1,0:T(8,128)(2,1)} %param.19) | copy-start | bytes 393220
  9.4 6.0 %collective-permute-start = (bf16[4,128,256]{2,1,0:T(8,128)(2,1)S(1)}, bf16[4,128,256]{2,1,0:T(8,128)(2,1)S(1)}, u32[]{:S(2)}, u32[]{:S(2)}) collective-permute-start(bf16[4,128,256]{2,1,0:T(8,128)(2,1)S(1)} %select_select_fusion), channel_id=1, source_target_pairs={{0,1},{1,2},{2,3},{3,4},{4,5},{5,6},{6,7},{7,0},{8,9},{9,10},{10,1... | collective-permute-start | bytes 786440 | tf_op jit(solution)/shard_map/ppermute | solution.py:24
  15.4 19.7 %copy-start.3 = (bf16[16,1,1,64,256]{4,3,2,1,0:T(8,128)(2,1)S(1)}, bf16[16,1,1,64,256]{4,3,2,1,0:T(8,128)(2,1)}, u32[]{:S(2)}) copy-start(bf16[16,1,1,64,256]{4,3,2,1,0:T(8,128)(2,1)} %param.23) | copy-start | bytes 1572868
  30.3 4.8 %copy-start.5 = (f32[4,256,256]{2,1,0:T(8,128)}, f32[4,256,256]{2,1,0:T(8,128)S(1)}, u32[]{:S(2)}) copy-start(f32[4,256,256]{2,1,0:T(8,128)S(1)} %get-tuple-element.428) | copy-start | bytes 3145732
  30.3 13.7 %copy-start.8 = (bf16[256,256]{1,0:T(8,128)(2,1)S(1)}, bf16[256,256]{1,0:T(8,128)(2,1)}, u32[]{:S(2)}) copy-start(bf16[256,256]{1,0:T(8,128)(2,1)} %param.21) | copy-start | bytes 393220
  30.3 5.8 %collective-permute-start.1 = (bf16[4,64,256]{2,1,0:T(8,128)(2,1)S(1)}, bf16[4,64,256]{2,1,0:T(8,128)(2,1)S(1)}, u32[]{:S(2)}, u32[]{:S(2)}) collective-permute-start(bf16[4,64,256]{2,1,0:T(8,128)(2,1)S(1)} %get-tuple-element.185), channel_id=1, source_target_pairs={{0,8},{8,16},{16,24},{24,0},{1,9},{9,17},{17,25},{25,1},{2,10},{10... | collective-permute-start | bytes 393224 | tf_op jit(solution)/shard_map/ppermute | solution.py:202
  31.7 11.7 %collective-permute-start.2 = (bf16[4,64,256]{2,1,0:T(8,128)(2,1)S(1)}, bf16[4,64,256]{2,1,0:T(8,128)(2,1)S(1)}, u32[]{:S(2)}, u32[]{:S(2)}) collective-permute-start(bf16[4,64,256]{2,1,0:T(8,128)(2,1)S(1)} %get-tuple-element.184), channel_id=1, source_target_pairs={{0,16},{8,24},{16,0},{24,8},{1,17},{9,25},{17,1},{25,9},{2,18},{10... | collective-permute-start | bytes 393224 | tf_op jit(solution)/shard_map/ppermute | solution.py:202
  34.0 9.3 %collective-permute-start.3 = (bf16[4,64,256]{2,1,0:T(8,128)(2,1)S(1)}, bf16[4,64,256]{2,1,0:T(8,128)(2,1)S(1)}, u32[]{:S(2)}, u32[]{:S(2)}) collective-permute-start(bf16[4,64,256]{2,1,0:T(8,128)(2,1)S(1)} %get-tuple-element.183), channel_id=1, source_target_pairs={{0,24},{8,0},{16,8},{24,16},{1,25},{9,1},{17,9},{25,17},{2,26},{10... | collective-permute-start | bytes 393224 | tf_op jit(solution)/shard_map/ppermute | solution.py:202
  44.3 3.2 %copy-start.7 = (bf16[256,256]{1,0:T(8,128)(2,1)S(1)}, bf16[256,256]{1,0:T(8,128)(2,1)}, u32[]{:S(2)}) copy-start(bf16[256,256]{1,0:T(8,128)(2,1)} %param.22) | copy-start | bytes 393220
  59.1 6.1 %copy-start.4 = (f32[64,4,16,16]{3,2,1,0:T(8,128)S(1)}, f32[64,4,16,16]{3,2,1,0:T(8,128)}, u32[]{:S(2)}) copy-start(f32[64,4,16,16]{3,2,1,0:T(8,128)} %fusion.52) | copy-start | bytes 786436
  81.4 1.8 %copy-start.9 = (bf16[256,256]{1,0:T(8,128)(2,1)S(1)}, bf16[256,256]{1,0:T(8,128)(2,1)}, u32[]{:S(2)}) copy-start(bf16[256,256]{1,0:T(8,128)(2,1)} %param.21) | copy-start | bytes 393220
  85.1 18.3 %all-to-all-start = ((bf16[16,64,256]{2,1,0:T(8,128)(2,1)}), bf16[16,64,256]{2,1,0:T(8,128)(2,1)S(1)}, u32[]{:S(2)}, u32[]{:S(2)}) async-start(bf16[16,64,256]{2,1,0:T(8,128)(2,1)} %bitcast.37), calls=%async_computation | async-start | bytes 1048576 | tf_op jit(solution)/shard_map/all_to_all | solution.py:207
  121.8 1.0 copy-start.6
  122.8 3.1 %collective-permute-start.5 = (f32[131072]{0:T(1024)S(1)}, f32[131072]{0:T(1024)S(1)}, u32[]{:S(2)}, u32[]{:S(2)}) collective-permute-start(f32[131072]{0:T(1024)S(1)} %broadcast_select_fusion), channel_id=1, source_target_pairs={{0,1},{1,0},{2,3},{3,2},{4,5},{5,4},{6,7},{7,6},{8,9},{9,8},{10,11... | collective-permute-start | bytes 1572872 | tf_op jit(solution)/shard_map/ppermute | solution.py:50
  126.0 31.7 %copy-start.11 = (bf16[4,128,256]{2,1,0:T(8,128)(2,1)S(1)}, bf16[4,128,256]{2,1,0:T(8,128)(2,1)}, u32[]{:S(2)}) copy-start(bf16[4,128,256]{2,1,0:T(8,128)(2,1)} %get-tuple-element.126) | copy-start | bytes 786436
  126.0 7.6 %collective-permute-start.6 = (f32[65536]{0:T(1024)S(1)}, f32[65536]{0:T(1024)S(1)}, u32[]{:S(2)}, u32[]{:S(2)}) collective-permute-start(f32[65536]{0:T(1024)S(1)} %slice_select_fusion), channel_id=1, source_target_pairs={{0,2},{1,3},{2,0},{3,1},{4,6},{5,7},{6,4},{7,5},{8,10},{9,11},{10,... | collective-permute-start | bytes 786440 | tf_op jit(solution)/shard_map/ppermute | solution.py:50
  127.3 45.2 %copy-start.10 = (s32[4,128]{1,0:T(4,128)S(1)}, s32[4,128]{1,0:T(4,128)}, u32[]{:S(2)}) copy-start(s32[4,128]{1,0:T(4,128)} %param.17) | copy-start | bytes 6148
  133.7 3.9 %collective-permute-start.7 = (f32[32768]{0:T(1024)S(1)}, f32[32768]{0:T(1024)S(1)}, u32[]{:S(2)}, u32[]{:S(2)}) collective-permute-start(f32[32768]{0:T(1024)S(1)} %slice_select_fusion.1), channel_id=1, source_target_pairs={{0,4},{1,5},{2,6},{3,7},{4,0},{5,1},{6,2},{7,3},{8,12},{9,13},{10,... | collective-permute-start | bytes 393224 | tf_op jit(solution)/shard_map/ppermute | solution.py:50
  137.6 3.2 %collective-permute-start.8 = (f32[16384]{0:T(1024)S(1)}, f32[16384]{0:T(1024)S(1)}, u32[]{:S(2)}, u32[]{:S(2)}) collective-permute-start(f32[16384]{0:T(1024)S(1)} %slice_select_fusion.2), channel_id=1, source_target_pairs={{0,8},{8,0},{16,24},{24,16},{1,9},{9,1},{17,25},{25,17},{2,10},{10... | collective-permute-start | bytes 196616 | tf_op jit(solution)/shard_map/ppermute | solution.py:50
  140.8 3.8 %collective-permute-start.9 = (f32[8192]{0:T(1024)S(1)}, f32[8192]{0:T(1024)S(1)}, u32[]{:S(2)}, u32[]{:S(2)}) collective-permute-start(f32[8192]{0:T(1024)S(1)} %slice_select_fusion.3), channel_id=1, source_target_pairs={{0,16},{8,24},{16,0},{24,8},{1,17},{9,25},{17,1},{25,9},{2,18},{10... | collective-permute-start | bytes 98312 | tf_op jit(solution)/shard_map/ppermute | solution.py:50
  144.6 4.7 %collective-permute-start.10 = (f32[8192]{0:T(1024)S(1)}, f32[8192]{0:T(1024)S(1)}, u32[]{:S(2)}, u32[]{:S(2)}) collective-permute-start(f32[8192]{0:T(1024)S(1)} %select_add_fusion.4), channel_id=1, source_target_pairs={{0,16},{8,24},{16,0},{24,8},{1,17},{9,25},{17,1},{25,9},{2,18},{10... | collective-permute-start | bytes 98312 | tf_op jit(solution)/shard_map/ppermute | solution.py:54
  149.3 3.2 %collective-permute-start.11 = (f32[16384]{0:T(1024)S(1)}, f32[16384]{0:T(1024)S(1)}, u32[]{:S(2)}, u32[]{:S(2)}) collective-permute-start(f32[16384]{0:T(1024)S(1)} %maximum_select_fusion.7), channel_id=1, source_target_pairs={{0,8},{8,0},{16,24},{24,16},{1,9},{9,1},{17,25},{25,17},{2,10},{10... | collective-permute-start | bytes 196616 | tf_op jit(solution)/shard_map/ppermute | solution.py:54
  152.5 3.9 %collective-permute-start.12 = (f32[32768]{0:T(1024)S(1)}, f32[32768]{0:T(1024)S(1)}, u32[]{:S(2)}, u32[]{:S(2)}) collective-permute-start(f32[32768]{0:T(1024)S(1)} %maximum_select_fusion.6), channel_id=1, source_target_pairs={{0,4},{1,5},{2,6},{3,7},{4,0},{5,1},{6,2},{7,3},{8,12},{9,13},{10,... | collective-permute-start | bytes 393224 | tf_op jit(solution)/shard_map/ppermute | solution.py:54
  156.4 9.1 %collective-permute-start.13 = (f32[65536]{0:T(1024)S(1)}, f32[65536]{0:T(1024)S(1)}, u32[]{:S(2)}, u32[]{:S(2)}) collective-permute-start(f32[65536]{0:T(1024)S(1)} %maximum_select_fusion.4), channel_id=1, source_target_pairs={{0,2},{1,3},{2,0},{3,1},{4,6},{5,7},{6,4},{7,5},{8,10},{9,11},{10,... | collective-permute-start | bytes 786440 | tf_op jit(solution)/shard_map/ppermute | solution.py:54
  157.6 14.8 %collective-permute-start.4 = (bf16[4,128,256]{2,1,0:T(8,128)(2,1)S(1)}, bf16[4,128,256]{2,1,0:T(8,128)(2,1)S(1)}, u32[]{:S(2)}, u32[]{:S(2)}) collective-permute-start(bf16[4,128,256]{2,1,0:T(8,128)(2,1)S(1)} %copy-done.11), channel_id=1, source_target_pairs={{0,7},{1,0},{2,1},{3,2},{4,3},{5,4},{6,5},{7,6},{8,15},{9,8},{10,9... | collective-permute-start | bytes 786440 | tf_op jit(solution)/shard_map/ppermute | solution.py:24
  165.5 8.7 %collective-permute-start.14 = (f32[131072]{0:T(1024)S(1)}, f32[131072]{0:T(1024)S(1)}, u32[]{:S(2)}, u32[]{:S(2)}) collective-permute-start(f32[131072]{0:T(1024)S(1)} %maximum_select_fusion.2), channel_id=1, source_target_pairs={{0,1},{1,0},{2,3},{3,2},{4,5},{5,4},{6,7},{7,6},{8,9},{9,8},{10,11... | collective-permute-start | bytes 1572872 | tf_op jit(solution)/shard_map/ppermute | solution.py:54
